TPU v7x, 32 devices: a whole 2x2x4 slice. The times are simulated.
32 devices in a mesh: section: 4 (over y, x), tp: 4 (over z), mirror: 2 (over core).
Axes of the slice: x: 2, y: 2, z: 4, core: 2. Of those that a mesh axis runs over, the one named last changes fastest.
Arguments:
- feats: bfloat16 [2, 2, 128, 5120], P('mirror', None, 'tp'), may hold values from -16 to 16
- types: int32 [2, 2, 128], P('mirror', None, 'tp'), may hold values from 0 to 63
- segs: int32 [2, 2, 5, 128], P('mirror'), may hold values from 0 to 3, never falling along the last dimension, each value on 1 to 64 neighbouring positions
- type_table: bfloat16 [64, 5120], replicated, may hold values from -3 to 3
- gains: float32 [2, 4, 5120], P('mirror', 'section'), may hold values from 0.25 to 1.75, as said below
- w_qkv: bfloat16 [2, 4, 3, 5120, 512], P('mirror', 'section', None, None, 'tp'), may hold values from -8 to 8, as said below
- w_out: bfloat16 [2, 4, 512, 5120], P('mirror', 'section', 'tp'), as said below
- carry_acts: bfloat16 [2, 4, 128, 5120], P('mirror', 'section', 'tp'), may hold values from -16 to 16
- grad_in: bfloat16 [2, 4, 128, 5120], P('mirror', 'section', 'tp'), may hold values from -6 to 6
- saved: bfloat16 [2, 4, 2, 128, 5120], P('mirror', 'section', None, 'tp'), may hold values from -16 to 16
- cotangent: bfloat16 [2, 2, 128, 5120], P('mirror', None, 'tp'), may hold values from -6 to 6
Outputs:
- acts: bfloat16 [2, 4, 2, 128, 5120], P('mirror', 'section', None, 'tp')
- grad_acts: bfloat16 [2, 4, 2, 128, 5120], P('mirror', 'section', None, 'tp')
- grad_qkv: bfloat16 [2, 4, 3, 5120, 512], P('mirror', 'section', None, None, 'tp')
- grad_out: bfloat16 [2, 4, 512, 5120], P('mirror', 'section', 'tp')
Inputs may be any that keep to these rules, and one draw needn't show every extreme that they name: w_qkv[1, k] equals w_qkv[0, 3 - k]. w_out[1, k] equals w_out[0, 3 - k]. gains[1, k] equals gains[0, 3 - k]. `segs`: segment numbers never fall along a micro-batch; each segment holds at most half of 128 tokens, and one holds exactly that many.
All inputs are finite; a program needn't handle non-finite values.
Results may differ from a plain program's by a relative error of at most 0.015.
Values may be sent and summed in bfloat16 or wider, within the bound.
No kernel may reach another device: no remote copies, remote signals or barrier semaphores. Data moves between devices by JAX's collectives and lax.ppermute only.
A program may use at most 128 MiB of HBM per device.

v0:
```python
import math
import numpy as np
import jax
import jax.numpy as jnp
from jax import lax
from jax.sharding import PartitionSpec as P

HD = 128


def passed_along(block, axis, distance):
    devices = range(lax.axis_size(axis))
    route = [(i - distance, i) for i in devices if i - distance in devices]
    return lax.ppermute(block, axis, route)


def flipped(value, axis, mask):
    return lax.ppermute(value, axis, [(i, i ^ mask) for i in range(lax.axis_size(axis))])


def normalize(values, gain_row):
    mean_square = jnp.mean(values * values, axis=-1, keepdims=True)
    return values * lax.rsqrt(mean_square + 1e-05) * gain_row


def segment_mask(segment_ids):
    position = jnp.arange(segment_ids.shape[0], dtype=jnp.int32)
    causal = position[None, :] <= position[:, None]
    return causal & (segment_ids[:, None] == segment_ids[None, :])


def attend(queries, keys_all, values_all, seg_mask):
    scores = jnp.einsum(
        "ihd,jhd->hij", queries, keys_all, preferred_element_type=jnp.float32
    ) / math.sqrt(queries.shape[-1])
    scores = jnp.where(seg_mask[None], scores, -1e30)
    highest = lax.stop_gradient(jnp.max(scores, axis=-1, keepdims=True))
    expo = jnp.exp(scores - highest)
    probs = (expo / jnp.sum(expo, axis=-1, keepdims=True)).astype(values_all.dtype)
    return jnp.einsum("hij,jhd->ihd", probs, values_all, preferred_element_type=jnp.float32)


def embedding(feat_rows, type_rows, type_table):
    onehot = (
        type_rows[:, None] == jnp.arange(type_table.shape[0], dtype=jnp.int32)[None, :]
    ).astype(jnp.bfloat16)
    looked = jnp.dot(onehot, type_table, preferred_element_type=jnp.float32)
    return (feat_rows.astype(jnp.float32) + looked).astype(jnp.bfloat16)


def gathered(blocks):
    full = lax.all_gather(jnp.stack(blocks), "tp", axis=1, tiled=True)
    return [full[i] for i in range(len(blocks))]


def scattered(blocks):
    part = lax.psum_scatter(jnp.stack(blocks), "tp", scatter_dimension=1, tiled=True)
    return [part[i] for i in range(len(blocks))]


def shards(
    feats, types, segs, type_table, gains, w_qkv, w_out, carry_acts, grad_in, saved, cotangent
):
    sections = lax.axis_size("section")
    section_index = lax.axis_index("section")
    on_first_pipe = lax.axis_index("mirror") == 0
    position = jnp.where(on_first_pipe, section_index, sections - 1 - section_index)
    gain_row = gains[0, 0]
    qkv_weight = w_qkv[0, 0]
    out_weight = w_out[0, 0]
    window_steps = feats.shape[1]
    seq_len = segs.shape[3]
    model_width = qkv_weight.shape[1]
    inner_here = qkv_weight.shape[-1]
    heads_here = inner_here // HD

    def mask_for(which, index):
        return segment_mask(lax.dynamic_index_in_dim(segs[0, which], index, 0, keepdims=False))

    def normed_rows(rows):
        return normalize(rows.astype(jnp.float32), gain_row).astype(jnp.bfloat16)

    def heads_of(normed_full):
        projected = jnp.einsum(
            "sd,cdn->csn", normed_full, qkv_weight, preferred_element_type=jnp.float32
        ).astype(jnp.bfloat16)
        return projected.reshape(3, seq_len, heads_here, HD)

    def forward_part(normed_full, seg_mask, heads_view=None):
        if heads_view is None:
            heads_view = heads_of(normed_full)
        mixed = (
            attend(heads_view[0], heads_view[1], heads_view[2], seg_mask)
            .reshape(seq_len, inner_here)
            .astype(jnp.bfloat16)
        )
        return mixed

    def backward_part(normed_full, upstream_full, seg_mask, heads_view=None):
        if heads_view is None:
            heads_view = heads_of(normed_full)
        primal, pull_attend = jax.vjp(
            lambda query_part, key_part, value_part: attend(
                query_part, key_part, value_part, seg_mask
            ),
            heads_view[0],
            heads_view[1],
            heads_view[2],
        )
        mixed = primal.reshape(seq_len, inner_here).astype(jnp.bfloat16)
        d_mixed = jnp.einsum(
            "sd,nd->sn", upstream_full, out_weight, preferred_element_type=jnp.float32
        ).astype(jnp.bfloat16)
        pulled = pull_attend(d_mixed.astype(jnp.float32).reshape(seq_len, heads_here, HD))
        d_projected = jnp.stack(pulled).reshape(3, seq_len, inner_here)
        return (d_projected, mixed)

    qkv_rows = jnp.transpose(qkv_weight, (0, 2, 1)).reshape(3 * inner_here, model_width)
    padded_out = jnp.concatenate(
        [out_weight, jnp.zeros((2 * inner_here, model_width), out_weight.dtype)], axis=0
    )
    block_weight = jnp.stack([qkv_rows, padded_out])

    def projected_back(d_projected, forward_mixed):
        lhs = jnp.stack(
            [
                jnp.transpose(d_projected, (1, 0, 2)).reshape(seq_len, 3 * inner_here),
                jnp.concatenate(
                    [forward_mixed, jnp.zeros((seq_len, 2 * inner_here), forward_mixed.dtype)],
                    axis=1,
                ),
            ]
        )
        return jnp.einsum(
            "tsk,tkd->tsd", lhs, block_weight, preferred_element_type=jnp.float32
        ).astype(jnp.bfloat16)

    def weight_terms(normed_fulls, d_projecteds, mixeds, upstream_fulls):
        qkv_sum = None
        out_sum = None
        for normed_full, d_projected, mixed, upstream_full in zip(
            normed_fulls, d_projecteds, mixeds, upstream_fulls
        ):
            qkv_term = jnp.einsum(
                "sd,csn->cdn", normed_full, d_projected, preferred_element_type=jnp.float32
            )
            out_term = jnp.einsum(
                "sn,sd->nd", mixed, upstream_full, preferred_element_type=jnp.float32
            )
            qkv_sum = qkv_term if qkv_sum is None else qkv_sum + qkv_term
            out_sum = out_term if out_sum is None else out_sum + out_term
        return (qkv_sum.astype(jnp.bfloat16), out_sum.astype(jnp.bfloat16))

    def input_grad(layer_in, upstream, d_normed):
        unused_norm, pull_norm = jax.vjp(
            lambda inputs: normalize(inputs, gain_row), layer_in.astype(jnp.float32)
        )
        d_input = pull_norm(d_normed.astype(jnp.float32))[0]
        return (upstream.astype(jnp.float32) + d_input).astype(jnp.bfloat16)

    pair_axes = ("section", "mirror")
    mirror_size = lax.axis_size("mirror")
    up_pairs = []
    down_pairs = []
    for section in range(sections):
        for mirror in range(mirror_size):
            ahead = 1 if mirror == 0 else -1
            if 0 <= section + ahead < sections:
                up_pairs.append(
                    (section * mirror_size + mirror, (section + ahead) * mirror_size + mirror)
                )
            if 0 <= section - ahead < sections:
                down_pairs.append(
                    (section * mirror_size + mirror, (section - ahead) * mirror_size + mirror)
                )
    bit_count = lax.axis_size(pair_axes).bit_length() - 1
    section_bits = list(range(1, bit_count))
    if section_bits:
        routes = []
        for start in range(len(section_bits)):
            order = section_bits[start:] + section_bits[:start]
            routes.append([1 | 1 << order[0]] + [1 << bit for bit in order[1:]])
    else:
        routes = [[1]]

    def to_partner(value):
        return flipped(value, pair_axes, (1 << bit_count) - 1)

    last_step = window_steps - 1
    saved_normed = [normed_rows(saved[0, 0, t]) for t in range(window_steps)]
    backward_normed_full = [None] * window_steps
    upstream_fulls = []
    d_projecteds = []
    mixeds = []
    partner_normed = [None] * window_steps
    partner_upstream = []
    partner_d_projected = []
    partner_mixed = []
    forward_outs = []
    backward_outs = []
    forward_in = carry_acts[0, 0]
    backward_in = grad_in[0, 0]
    inbox = {}
    deferred = {}
    tie_scatter = {}
    for step_index in range(window_steps):
        embedded = embedding(feats[0, step_index], types[0, step_index], type_table)
        current = jnp.where(position == 0, embedded, forward_in)
        upstream = jnp.where(position == sections - 1, cotangent[0, step_index], backward_in)
        if step_index == 0:
            upstream_full, backward_normed_full[0], forward_normed_full = gathered(
                [upstream, saved_normed[0], normed_rows(current)]
            )
            first_sent = to_partner(jnp.stack([upstream_full, backward_normed_full[0]]))
            paired = jnp.einsum(
                "tsd,cdn->tcsn",
                jnp.stack([backward_normed_full[0], forward_normed_full]),
                qkv_weight,
                preferred_element_type=jnp.float32,
            ).astype(jnp.bfloat16)
            step_heads = [paired[t].reshape(3, seq_len, heads_here, HD) for t in range(2)]
        else:
            step_heads = [None, None]
            upstream_full, forward_normed_full = gathered([upstream, normed_rows(current)])
            inbox[f"rows{step_index}"] = to_partner(upstream_full)
        d_projected, mixed = backward_part(
            backward_normed_full[step_index],
            upstream_full,
            mask_for(1, step_index + position),
            step_heads[0],
        )
        upstream_fulls.append(upstream_full)
        d_projecteds.append(d_projected)
        mixeds.append(mixed)
        small = jnp.concatenate([d_projected, mixed[None]])
        if step_index < last_step:
            deferred[f"small{step_index}"] = small
        else:
            inbox[f"small{step_index}"] = to_partner(small)
        forward_mixed = forward_part(
            forward_normed_full, mask_for(0, step_index - position + sections - 1), step_heads[1]
        )
        both_parts, tie_scatter = lax.optimization_barrier(
            (projected_back(d_projected, forward_mixed), tie_scatter)
        )
        inbox.update(tie_scatter)
        tie_scatter = {}
        both_rows = lax.psum_scatter(both_parts, "tp", scatter_dimension=1, tiled=True)
        d_normed, attn_rows = (both_rows[0], both_rows[1])
        if step_index == 0 and window_steps > 1:
            later_rows, d_normed = lax.optimization_barrier((saved_normed[1:], d_normed))
            later = gathered(later_rows)
            backward_normed_full[1:] = later
            deferred["later"] = jnp.stack(later)
        backward_out = input_grad(saved[0, 0, step_index], upstream, d_normed)
        forward_out = (current.astype(jnp.float32) + attn_rows.astype(jnp.float32)).astype(
            jnp.bfloat16
        )
        forward_outs.append(forward_out)
        backward_outs.append(backward_out)
        if step_index < last_step:
            backward_in = lax.ppermute(backward_out, pair_axes, down_pairs)
            forward_in = lax.ppermute(forward_out, pair_axes, up_pairs)
            if step_index == 0:
                deferred, first_sent, backward_in, forward_in = lax.optimization_barrier(
                    (deferred, first_sent, backward_in, forward_in)
                )
                inbox["first"] = first_sent
            else:
                deferred, backward_in, forward_in = lax.optimization_barrier(
                    (deferred, backward_in, forward_in)
                )
            tie_scatter = {key: to_partner(value) for key, value in deferred.items()}
            deferred = {}
    partner_upstream = [inbox["first"][0]] + [inbox[f"rows{t}"] for t in range(1, window_steps)]
    partner_normed = [inbox["first"][1]] + (
        [inbox["later"][t] for t in range(window_steps - 1)] if window_steps > 1 else []
    )
    partner_d_projected = [inbox[f"small{t}"][:3] for t in range(window_steps)]
    partner_mixed = [inbox[f"small{t}"][3] for t in range(window_steps)]
    own_qkv, own_out = weight_terms(backward_normed_full, d_projecteds, mixeds, upstream_fulls)
    other_qkv, other_out = weight_terms(
        partner_normed, partner_d_projected, partner_mixed, partner_upstream
    )
    grad_qkv = (own_qkv.astype(jnp.float32) + other_qkv.astype(jnp.float32)).astype(jnp.bfloat16)
    grad_out = (own_out.astype(jnp.float32) + other_out.astype(jnp.float32)).astype(jnp.bfloat16)
    acts_block = jnp.stack(forward_outs)[None, None]
    grads_block = jnp.stack(backward_outs)[None, None]
    return (acts_block, grads_block, grad_qkv[None, None], grad_out[None, None])


def solution(mesh):
    in_specs = (
        P("mirror", None, "tp", None),
        P("mirror", None, "tp"),
        P("mirror", None, None, None),
        P(),
        P("mirror", "section", None),
        P("mirror", "section", None, None, "tp"),
        P("mirror", "section", "tp", None),
        P("mirror", "section", "tp", None),
        P("mirror", "section", "tp", None),
        P("mirror", "section", None, "tp", None),
        P("mirror", None, "tp", None),
    )
    out_specs = (
        P("mirror", "section", None, "tp", None),
        P("mirror", "section", None, "tp", None),
        P("mirror", "section", None, None, "tp"),
        P("mirror", "section", "tp", None),
    )
    return jax.shard_map(shards, mesh=mesh, in_specs=in_specs, out_specs=out_specs, check_vma=False)
```

profile of v0, /device:TPU:0, one launch (start us, length us, event | category | flops | bytes accessed | tf_op | source)
XLA Modules:
  0.0 318.5 jit_solution(18364899609434030031)
XLA Ops:
  13.8 6.3 %copy.15 = bf16[3,128,5120]{2,1,0:T(8,128)(2,1)} copy(bf16[3,128,5120]{1,2,0:T(8,128)(2,1)} %bitcast.361) | data formatting | bytes 7864320 | tf_op jit(solution)/shard_map/transpose | solution.py:118
  20.6 3.7 %pad_bitcast_fusion = bf16[1,384,5120]{2,1,0:T(8,128)(2,1)} fusion(bf16[128,5120]{1,0:T(8,128)(2,1)} %bitcast.363), kind=kLoop, calls=%fused_computation.28 | loop fusion | bytes 5242880 | tf_op jit(solution)/shard_map/stack | solution.py:122
  24.3 68.7 %all-gather.5.cloned.1.call-done = bf16[3,128,5120]{2,1,0:T(8,128)(2,1)} async-done(((bf16[3,32,5120]{2,1,0:T(8,128)(2,1)}), bf16[3,128,5120]{2,1,0:T(8,128)(2,1)}) %all-gather.5.cloned.1.call-update) | async-done | bytes 3932176 | tf_op jit(solution)/shard_map/all_gather | solution.py:52
  93.0 4.6 %fusion.33 = bf16[2,3,128,128]{3,2,1,0:T(8,128)(2,1)S(1)} fusion(bf16[1,1,3,5120,128]{4,3,2,1,0:T(8,128)(2,1)} %param.16, bf16[3,128,5120]{2,1,0:T(8,128)(2,1)} %all-gather.5.cloned.1.call-done), kind=kOutput, calls=%fused_computation.47 | convolution fusion | flops 1006731264 | bytes 6750208 | tf_op jit(solution)/shard_map/tsd,cdn->tcsn/dot_general | solution.py:215
  97.9 2.0 fusion.68
  101.3 3.0 convolution_convert_fusion.1
  105.6 3.5 %stack.115 = bf16[2,128,5120]{2,1,0:T(8,128)(2,1)} slice(bf16[3,128,5120]{2,1,0:T(8,128)(2,1)} %all-gather.5.cloned.1.call-done), slice={[0:2], [0:128], [0:5120]} | slice | bytes 5242880 | tf_op jit(solution)/shard_map/stack | solution.py:214
  110.8 44.5 %reduce-scatter.3.cloned.1.call-done = bf16[2,32,5120]{2,1,0:T(8,128)(2,1)} async-done(((bf16[2,128,5120]{2,1,0:T(8,128)(2,1)}), bf16[2,32,5120]{2,1,0:T(8,128)(2,1)}) %reduce-scatter.3.cloned.1.call-update) | async-done | bytes 655376 | tf_op jit(solution)/shard_map/reduce_scatter | solution.py:248
  159.2 5.3 %collective-permute-start.2 = (bf16[32,5120]{1,0:T(8,128)(2,1)S(1)}, bf16[32,5120]{1,0:T(8,128)(2,1)}, u32[]{:S(2)}, u32[]{:S(2)}) collective-permute-start(bf16[32,5120]{1,0:T(8,128)(2,1)S(1)} %fusion.90), channel_id=1, source_target_pairs={{0,8},{8,16},{9,1},{16,24},{17,9},{25,17},{2,10},{10,18},{11,3},{1... | collective-permute-start | bytes 983048 | tf_op jit(solution)/shard_map/ppermute | solution.py:263
  166.1 3.3 %collective-permute-done = bf16[2,128,5120]{2,1,0:T(8,128)(2,1)} collective-permute-done((bf16[2,128,5120]{2,1,0:T(8,128)(2,1)}, bf16[2,128,5120]{2,1,0:T(8,128)(2,1)}, u32[]{:S(2)}, u32[]{:S(2)}) %collective-permute-start) | collective-permute-done | bytes 2621472 | tf_op jit(solution)/shard_map/ppermute | solution.py:18
  169.4 6.7 %collective-permute-done.1 = bf16[32,5120]{1,0:T(8,128)(2,1)S(1)} collective-permute-done((bf16[32,5120]{1,0:T(8,128)(2,1)S(1)}, bf16[32,5120]{1,0:T(8,128)(2,1)S(1)}, u32[]{:S(2)}, u32[]{:S(2)}) %collective-permute-start.1) | collective-permute-done | bytes 327712 | tf_op jit(solution)/shard_map/ppermute | solution.py:262
  176.1 13.3 %all-gather.9.cloned.1.call-done = bf16[128,5120]{1,0:T(8,128)(2,1)} async-done(((bf16[32,5120]{1,0:T(8,128)(2,1)}), bf16[128,5120]{1,0:T(8,128)(2,1)}) %all-gather.9.cloned.1.call-update) | async-done | bytes 1310736 | tf_op jit(solution)/shard_map/all_gather | solution.py:52
  193.8 3.0 fusion.44
  197.0 48.9 %all-gather.7.cloned.1.call-done = bf16[2,128,5120]{2,1,0:T(8,128)(2,1)} async-done(((bf16[2,32,5120]{2,1,0:T(8,128)(2,1)}), bf16[2,128,5120]{2,1,0:T(8,128)(2,1)}) %all-gather.7.cloned.1.call-update) | async-done | bytes 2621456 | tf_op jit(solution)/shard_map/all_gather | solution.py:52
  248.1 3.5 %fusion.49 = bf16[3,128,128]{2,1,0:T(8,128)(2,1)S(1)} fusion(bf16[1,1,3,5120,128]{4,3,2,1,0:T(8,128)(2,1)} %param.16, bf16[2,128,5120]{2,1,0:T(8,128)(2,1)} %all-gather.7.cloned.1.call-done), kind=kOutput, calls=%fused_computation.55 | convolution fusion | flops 503365632 | bytes 5341184 | tf_op jit(solution)/shard_map/sd,cdn->csn/dot_general | solution.py:84
  252.9 3.0 convolution_convert_fusion
  258.5 2.6 fusion.18
  266.9 3.4 %fusion.19 = f32[128,5120]{1,0:T(8,128)} fusion(bf16[2,128,5120]{2,1,0:T(8,128)(2,1)} %collective-permute-done, bf16[4,128,128]{1,2,0:T(8,128)(2,1)S(1)} %collective-permute-done.4), kind=kOutput, calls=%fused_computation.35 | convolution fusion | flops 167772160 | bytes 3964928 | tf_op jit(solution)/shard_map/sn,sd->nd/dot_general | solution.py:147
  270.3 2.5 fusion.21
  272.8 4.4 %fusion = bf16[1,1,3,5120,128]{3,4,2,1,0:T(8,128)(2,1)} fusion(f32[3,128,5120]{2,1,0:T(8,128)S(1)} %fusion.21, bf16[4,128,128]{1,2,0:T(8,128)(2,1)S(1)} %collective-permute-done.4, bf16[3,128,5120]{2,1,0:T(8,128)(2,1)S(1)} %add_convert_fusion.2, bf16[2,128,5120]{2,1,0:T(8,128)(2,1)} %collective-permute-done), kind=kOutput, calls=%fused_computation.6 | convolution fusion | flops 515112960 | bytes 17170432 | tf_op jit(solution)/shard_map/sd,csn->cdn/dot_general | solution.py:144
  277.3 6.3 %copy.18 = bf16[1,1,3,5120,128]{4,3,2,1,0:T(8,128)(2,1)} copy(bf16[1,1,3,5120,128]{3,4,2,1,0:T(8,128)(2,1)} %fusion) | data formatting | bytes 7864320
  283.5 11.9 %collective-permute-done.6 = bf16[128,5120]{1,0:T(8,128)(2,1)} collective-permute-done((bf16[128,5120]{1,0:T(8,128)(2,1)}, bf16[128,5120]{1,0:T(8,128)(2,1)}, u32[]{:S(2)}, u32[]{:S(2)}) %collective-permute-start.6) | collective-permute-done | bytes 1310752 | tf_op jit(solution)/shard_map/ppermute | solution.py:18
  295.4 3.8 %fusion.7 = bf16[1,1,128,5120]{3,2,1,0:T(8,128)(2,1)} fusion(f32[128,5120]{1,0:T(8,128)S(1)} %fusion.6, f32[128,5120]{1,0:T(8,128)} %fusion.19, bf16[128,5120]{1,0:T(8,128)(2,1)} %collective-permute-done.6, bf16[4,128,128]{1,2,0:T(8,128)(2,1)S(1)} %collective-permute-done.5), kind=kOutput, calls=%fused_computation.15 | convolution fusion | flops 171048960 | bytes 7897088 | tf_op jit(solution)/shard_map/sn,sd->nd/dot_general | solution.py:147
  299.2 7.9 %reduce-scatter.5.cloned.1.call-done = bf16[2,32,5120]{2,1,0:T(8,128)(2,1)} async-done(((bf16[2,128,5120]{2,1,0:T(8,128)(2,1)}), bf16[2,32,5120]{2,1,0:T(8,128)(2,1)}) %reduce-scatter.5.cloned.1.call-update) | async-done | bytes 655376 | tf_op jit(solution)/shard_map/reduce_scatter | solution.py:248
  (142 shorter events, 38.1 us)
Async XLA Ops:
  7.2 85.8 %all-gather.5.cloned.1.call-start = ((), (), s32[]{:S(2)}) async-start(), calls=%async_computation.2 | async-start | bytes 4915200 | tf_op jit(solution)/shard_map/all_gather | solution.py:52
  13.7 141.5 %reduce-scatter.3.cloned.1.call-start = ((), (), s32[]{:S(2)}) async-start(), calls=%async_computation.3 | async-start | bytes 3276800 | tf_op jit(solution)/shard_map/reduce_scatter | solution.py:248
  13.8 6.3 %copy-start.27 = (s32[1,2,5,128]{3,1,2,0:T(2,128)S(1)}, s32[1,2,5,128]{3,1,2,0:T(2,128)}, u32[]{:S(2)}) copy-start(s32[1,2,5,128]{3,1,2,0:T(2,128)} %param.13) | copy-start | bytes 15364
  93.0 8.3 %copy-start.4 = (bf16[1,384,5120]{2,1,0:T(8,128)(2,1)S(1)}, bf16[1,384,5120]{2,1,0:T(8,128)(2,1)}, u32[]{:S(2)}) copy-start(bf16[1,384,5120]{2,1,0:T(8,128)(2,1)} %pad_bitcast_fusion) | copy-start | bytes 11796484
  104.3 85.2 %all-gather.9.cloned.1.call-start = ((), (), s32[]{:S(2)}) async-start(), calls=%async_computation.6 | async-start | bytes 1638400 | tf_op jit(solution)/shard_map/all_gather | solution.py:52
  109.1 60.3 %collective-permute-start = (bf16[2,128,5120]{2,1,0:T(8,128)(2,1)}, bf16[2,128,5120]{2,1,0:T(8,128)(2,1)}, u32[]{:S(2)}, u32[]{:S(2)}) collective-permute-start(bf16[2,128,5120]{2,1,0:T(8,128)(2,1)} %stack.115), channel_id=1, source_target_pairs={{0,25},{1,24},{8,17},{9,16},{16,9},{17,8},{24,1},{25,0},{2,27},{3,... | collective-permute-start | bytes 7864328 | tf_op jit(solution)/shard_map/ppermute | solution.py:18
  156.3 89.7 %all-gather.7.cloned.1.call-start = ((), (), s32[]{:S(2)}) async-start(), calls=%async_computation.4 | async-start | bytes 3276800 | tf_op jit(solution)/shard_map/all_gather | solution.py:52
  156.8 32.9 %copy-start.18 = (bf16[32,5120]{1,0:T(8,128)(2,1)}, bf16[32,5120]{1,0:T(8,128)(2,1)S(1)}, u32[]{:S(2)}) copy-start(bf16[32,5120]{1,0:T(8,128)(2,1)S(1)} %fusion.78) | copy-start | bytes 983044
  156.9 19.3 %collective-permute-start.1 = (bf16[32,5120]{1,0:T(8,128)(2,1)S(1)}, bf16[32,5120]{1,0:T(8,128)(2,1)S(1)}, u32[]{:S(2)}, u32[]{:S(2)}) collective-permute-start(bf16[32,5120]{1,0:T(8,128)(2,1)S(1)} %fusion.78), channel_id=1, source_target_pairs={{1,9},{8,0},{9,17},{16,8},{17,25},{24,16},{3,11},{10,2},{11,19},{1... | collective-permute-start | bytes 983048 | tf_op jit(solution)/shard_map/ppermute | solution.py:262
  159.2 30.3 %copy-start.15 = (bf16[32,5120]{1,0:T(8,128)(2,1)}, bf16[32,5120]{1,0:T(8,128)(2,1)S(1)}, u32[]{:S(2)}) copy-start(bf16[32,5120]{1,0:T(8,128)(2,1)S(1)} %fusion.90) | copy-start | bytes 983044
  159.2 16.9 %collective-permute-start.2 = (bf16[32,5120]{1,0:T(8,128)(2,1)S(1)}, bf16[32,5120]{1,0:T(8,128)(2,1)}, u32[]{:S(2)}, u32[]{:S(2)}) collective-permute-start(bf16[32,5120]{1,0:T(8,128)(2,1)S(1)} %fusion.90), channel_id=1, source_target_pairs={{0,8},{8,16},{9,1},{16,24},{17,9},{25,17},{2,10},{10,18},{11,3},{1... | collective-permute-start | bytes 983048 | tf_op jit(solution)/shard_map/ppermute | solution.py:263
  165.4 10.7 %copy-start.24 = (bf16[128,128]{1,0:T(8,128)(2,1)}, bf16[128,128]{1,0:T(8,128)(2,1)S(1)}, u32[]{:S(2)}) copy-start(bf16[128,128]{1,0:T(8,128)(2,1)S(1)} %convolution_convert_fusion.8) | copy-start | bytes 98308
  176.1 14.7 %copy-start.20 = (bf16[32,5120]{1,0:T(8,128)(2,1)}, bf16[32,5120]{1,0:T(8,128)(2,1)S(1)}, u32[]{:S(2)}) copy-start(bf16[32,5120]{1,0:T(8,128)(2,1)S(1)} %collective-permute-done.1) | copy-start | bytes 983044
  189.7 7.1 %copy-start.10 = (bf16[32,5120]{1,0:T(8,128)(2,1)}, bf16[32,5120]{1,0:T(8,128)(2,1)S(1)}, u32[]{:S(2)}) copy-start(bf16[32,5120]{1,0:T(8,128)(2,1)S(1)} %get-tuple-element.31) | copy-start | bytes 983044
  190.9 55.1 %copy-start.14 = (bf16[1,1,128,5120]{3,2,1,0:T(8,128)(2,1)S(1)}, bf16[1,1,128,5120]{3,2,1,0:T(8,128)(2,1)}, u32[]{:S(2)}) copy-start(bf16[1,1,128,5120]{3,2,1,0:T(8,128)(2,1)} %param.17) | copy-start | bytes 3932164
  190.9 116.2 %reduce-scatter.5.cloned.1.call-start = ((), (), s32[]{:S(2)}) async-start(), calls=%async_computation.5 | async-start | bytes 3276800 | tf_op jit(solution)/shard_map/reduce_scatter | solution.py:248
  191.1 64.8 %collective-permute-start.3 = (bf16[1,128,5120]{2,1,0:T(8,128)(2,1)S(1)}, bf16[1,128,5120]{2,1,0:T(8,128)(2,1)}, u32[]{:S(2)}, u32[]{:S(2)}) collective-permute-start(bf16[1,128,5120]{2,1,0:T(8,128)(2,1)S(1)} %bitcast.362), channel_id=1, source_target_pairs={{0,25},{1,24},{8,17},{9,16},{16,9},{17,8},{24,1},{25,0},{2,27},{3,... | collective-permute-start | bytes 3932168 | tf_op jit(solution)/shard_map/ppermute | solution.py:18
  192.3 63.6 %collective-permute-start.4 = (bf16[4,128,128]{1,2,0:T(8,128)(2,1)}, bf16[4,128,128]{1,2,0:T(8,128)(2,1)S(1)}, u32[]{:S(2)}, u32[]{:S(2)}) collective-permute-start(bf16[4,128,128]{1,2,0:T(8,128)(2,1)} %pad_maximum_fusion.5), channel_id=1, source_target_pairs={{0,25},{1,24},{8,17},{9,16},{16,9},{17,8},{24,1},{25,0},{2,27},{3,... | collective-permute-start | bytes 393224 | tf_op jit(solution)/shard_map/ppermute | solution.py:18
  246.0 6.9 %copy-start.5 = (bf16[1,384,5120]{2,1,0:T(8,128)(2,1)S(1)}, bf16[1,384,5120]{2,1,0:T(8,128)(2,1)}, u32[]{:S(2)}) copy-start(bf16[1,384,5120]{2,1,0:T(8,128)(2,1)} %pad_bitcast_fusion) | copy-start | bytes 11796484
  261.3 9.0 %collective-permute-start.5 = (bf16[4,128,128]{1,2,0:T(8,128)(2,1)S(1)}, bf16[4,128,128]{1,2,0:T(8,128)(2,1)S(1)}, u32[]{:S(2)}, u32[]{:S(2)}) collective-permute-start(bf16[4,128,128]{1,2,0:T(8,128)(2,1)S(1)} %pad_maximum_fusion.6), channel_id=1, source_target_pairs={{0,25},{1,24},{8,17},{9,16},{16,9},{17,8},{24,1},{25,0},{2,27},{3,... | collective-permute-start | bytes 393224 | tf_op jit(solution)/shard_map/ppermute | solution.py:18
  264.2 31.3 %collective-permute-start.6 = (bf16[128,5120]{1,0:T(8,128)(2,1)}, bf16[128,5120]{1,0:T(8,128)(2,1)}, u32[]{:S(2)}, u32[]{:S(2)}) collective-permute-start(bf16[128,5120]{1,0:T(8,128)(2,1)} %slice_bitcast_fusion.6), channel_id=1, source_target_pairs={{0,25},{1,24},{8,17},{9,16},{16,9},{17,8},{24,1},{25,0},{2,27},{3,... | collective-permute-start | bytes 3932168 | tf_op jit(solution)/shard_map/ppermute | solution.py:18
  283.5 23.6 %copy-start.7 = (bf16[1,1,2,32,5120]{4,3,2,1,0:T(8,128)(2,1)S(1)}, bf16[1,1,2,32,5120]{4,3,2,1,0:T(8,128)(2,1)}, u32[]{:S(2)}) copy-start(bf16[1,1,2,32,5120]{4,3,2,1,0:T(8,128)(2,1)} %param.20) | copy-start | bytes 1966084
  299.2 11.0 %copy-start.19 = (bf16[32,5120]{1,0:T(8,128)(2,1)S(1)}, bf16[32,5120]{1,0:T(8,128)(2,1)}, u32[]{:S(2)}) copy-start(bf16[32,5120]{1,0:T(8,128)(2,1)} %copy-done.18) | copy-start | bytes 983044
  299.2 11.9 %copy-start.16 = (bf16[32,5120]{1,0:T(8,128)(2,1)S(1)}, bf16[32,5120]{1,0:T(8,128)(2,1)}, u32[]{:S(2)}) copy-start(bf16[32,5120]{1,0:T(8,128)(2,1)} %copy-done.15) | copy-start | bytes 983044
  (17 other events, 58.8 us)
Sparse Core Ops, SparseCore 0:
  13.8 79.1 all-gather.4
  104.4 50.7 reduce-scatter.2
  157.4 32.0 all-gather.8
  191.5 54.4 all-gather.6
  256.0 51.0 reduce-scatter.4
where the time goes:
time: 320 us; the launch traced here: 319 us
  waiting for transfers between devices  205 us (64%)
  matrix products  47.8 us (15%)
  local copies, waits for them, and re-layouts  24.6 us (8%)
  between operations  14.4 us (4%)
  starting transfers between devices  14.1 us (4%)
  other arithmetic  12.3 us (4%)
    all_gather x3, waiting for transfers between devices, gathered(): full = lax.all_gather(jnp.stack(blocks), 'tp', axis=1, tiled=True)  131 us
    reduce_scatter x2, waiting for transfers between devices, shards(): lax.psum_scatter(both_parts, 'tp', scatter_dimension=1, tiled=True)  52.4 us
    ppermute x5, waiting for transfers between devices, flipped(): lax.ppermute(value, axis, [(i, i ^ mask) for i in range(lax.axis_size(axi...  15.3 us
    dot_general x4, matrix products, weight_terms(): jnp.einsum('sd,csn->cdn', normed_full, d_projected, preferred_element_typ...  10.7 us
    dot_general x4, matrix products, weight_terms(): jnp.einsum('sn,sd->nd', mixed, upstream_full, preferred_element_type=jnp....  9.49 us
    unnamed x59, local copies, waits for them, and re-layouts  7.12 us
    ppermute x5, starting transfers between devices, flipped(): lax.ppermute(value, axis, [(i, i ^ mask) for i in range(lax.axis_size(axi...  7.08 us
    ppermute x1, waiting for transfers between devices, shards(): backward_in = lax.ppermute(backward_out, pair_axes, down_pairs)  6.69 us
  transfers between devices with their start and end apart: 12, of which 8 were waited for; matrix products, arithmetic and copies ran while one was open for 19% of the time, Pallas kernels for 0%

commit v1 on v0

--- a/solution.py
+++ b/solution.py
@@ -6,6 +6,18 @@
 from jax.sharding import PartitionSpec as P
 
 HD = 128
+
+
+def gather_by_bits(shard, axis, dim):
+    ways, here = (lax.axis_size(axis), lax.axis_index(axis))
+    grown, reach = (shard, 1)
+    while reach < ways:
+        theirs = lax.ppermute(grown, axis, [(d, d ^ reach) for d in range(ways)])
+        mine_first = jnp.concatenate([grown, theirs], axis=dim)
+        theirs_first = jnp.concatenate([theirs, grown], axis=dim)
+        grown = jnp.where(here & reach == 0, mine_first, theirs_first)
+        reach = 2 * reach
+    return grown
 
 
 def passed_along(block, axis, distance):
@@ -49,7 +61,7 @@
 
 
 def gathered(blocks):
-    full = lax.all_gather(jnp.stack(blocks), "tp", axis=1, tiled=True)
+    full = gather_by_bits(jnp.stack(blocks), "tp", 1)
     return [full[i] for i in range(len(blocks))]
 
 

time: 320 us -> 383 us (1.20)
  waiting for transfers between devices: 205 us -> 264 us
  matrix products: 47.8 us -> 38.2 us
  starting transfers between devices: 14.1 us -> 20.9 us
  other arithmetic: 12.3 us -> 17.5 us
    ppermute x0 -> x6, waiting for transfers between devices: none -> 200 us  [gather_by_bits(): theirs = lax.ppermute(grown, axis, [(d, d ^ reach) for d in range(ways)])]
    all_gather x3 -> x0, waiting for transfers between devices: 131 us -> none  [gathered(): full = lax.all_gather(jnp.stack(blocks), 'tp', axis=1, tiled=True)]
    ppermute x0 -> x6, starting transfers between devices: none -> 9.72 us  [gather_by_bits(): theirs = lax.ppermute(grown, axis, [(d, d ^ reach) for d in range(ways)])]
    select_n x0 -> x7, other arithmetic: none -> 7.67 us  [gather_by_bits(): grown = jnp.where(here & reach == 0, mine_first, theirs_first)]
    ppermute x1, waiting for transfers between devices: 6.69 us -> 0.01 us  [shards(): backward_in = lax.ppermute(backward_out, pair_axes, down_pairs)]
    dot_general x2, matrix products: 6.45 us -> 1.73 us  [heads_of(): jnp.einsum('sd,cdn->csn', normed_full, qkv_weight, preferred_element_type...]
    ppermute x5, waiting for transfers between devices: 15.3 us -> 11 us  [flipped(): lax.ppermute(value, axis, [(i, i ^ mask) for i in range(lax.axis_size(axi...]
    unnamed x59 -> x95, local copies, waits for them, and re-layouts: 7.12 us -> 11.3 us
  transfers between devices with their start and end apart: 12 -> 15, of which waited for: 8 -> 9; matrix products, arithmetic and copies ran while one was open for 19% -> 14% of each run, Pallas kernels for 0% -> 0%
where the time goes in v1:
time: 383 us; the launch traced here: 382 us
  waiting for transfers between devices  264 us (69%)
  matrix products  38.2 us (10%)
  local copies, waits for them, and re-layouts  26.1 us (7%)
  starting transfers between devices  20.9 us (5%)
  other arithmetic  17.5 us (5%)
  between operations  14.9 us (4%)
    ppermute x6, waiting for transfers between devices, gather_by_bits(): theirs = lax.ppermute(grown, axis, [(d, d ^ reach) for d in range(ways)])  200 us
    reduce_scatter x2, waiting for transfers between devices, shards(): lax.psum_scatter(both_parts, 'tp', scatter_dimension=1, tiled=True)  53.4 us
    unnamed x95, local copies, waits for them, and re-layouts  11.3 us
    ppermute x5, waiting for transfers between devices, flipped(): lax.ppermute(value, axis, [(i, i ^ mask) for i in range(lax.axis_size(axi...  11 us
    dot_general x4, matrix products, weight_terms(): jnp.einsum('sn,sd->nd', mixed, upstream_full, preferred_element_type=jnp....  10.8 us
    dot_general x4, matrix products, weight_terms(): jnp.einsum('sd,csn->cdn', normed_full, d_projected, preferred_element_typ...  10.8 us
    ppermute x6, starting transfers between devices, gather_by_bits(): theirs = lax.ppermute(grown, axis, [(d, d ^ reach) for d in range(ways)])  9.72 us
    select_n x7, other arithmetic, gather_by_bits(): grown = jnp.where(here & reach == 0, mine_first, theirs_first)  7.67 us
  transfers between devices with their start and end apart: 15, of which 9 were waited for; matrix products, arithmetic and copies ran while one was open for 14% of the time, Pallas kernels for 0%

profile of v1, /device:TPU:0, one launch (start us, length us, event | category | flops | bytes accessed | tf_op | source)
XLA Modules:
  0.0 381.8 jit_solution(5801120682936594483)
XLA Ops:
  13.4 3.1 collective-permute-start
  16.5 21.9 %collective-permute-done = bf16[3,32,5120]{2,1,0:T(8,128)(2,1)} collective-permute-done((bf16[3,32,5120]{2,1,0:T(8,128)(2,1)S(1)}, bf16[3,32,5120]{2,1,0:T(8,128)(2,1)}, u32[]{:S(2)}, u32[]{:S(2)}) %collective-permute-start) | collective-permute-done | bytes 983072 | tf_op jit(solution)/shard_map/ppermute | solution.py:15
  38.4 2.4 maximum_select_fusion.2
  40.8 2.8 collective-permute-start.1
  43.7 6.4 %copy.15 = bf16[3,128,5120]{2,1,0:T(8,128)(2,1)} copy(bf16[3,128,5120]{1,2,0:T(8,128)(2,1)} %bitcast.360) | data formatting | bytes 7864320 | tf_op jit(solution)/shard_map/transpose | solution.py:130
  51.8 76.2 %collective-permute-done.1 = bf16[3,64,5120]{2,1,0:T(8,128)(2,1)} collective-permute-done((bf16[3,64,5120]{2,1,0:T(8,128)(2,1)S(1)}, bf16[3,64,5120]{2,1,0:T(8,128)(2,1)}, u32[]{:S(2)}, u32[]{:S(2)}) %collective-permute-start.1) | collective-permute-done | bytes 1966112 | tf_op jit(solution)/shard_map/ppermute | solution.py:15
  128.0 2.8 maximum_select_fusion
  135.3 3.0 convolution_convert_fusion.1
  139.7 3.6 stack.115
  145.9 45.9 %reduce-scatter.3.cloned.1.call-done = bf16[2,32,5120]{2,1,0:T(8,128)(2,1)} async-done(((bf16[2,128,5120]{2,1,0:T(8,128)(2,1)}), bf16[2,32,5120]{2,1,0:T(8,128)(2,1)}) %reduce-scatter.3.cloned.1.call-update) | async-done | bytes 655376 | tf_op jit(solution)/shard_map/reduce_scatter | solution.py:260
  195.3 6.7 %collective-permute-done.2 = bf16[1,32,5120]{2,1,0:T(8,128)(2,1)S(1)} collective-permute-done((bf16[1,32,5120]{2,1,0:T(8,128)(2,1)S(1)}, bf16[1,32,5120]{2,1,0:T(8,128)(2,1)S(1)}, u32[]{:S(2)}, u32[]{:S(2)}) %collective-permute-start.2) | collective-permute-done | bytes 327712 | tf_op jit(solution)/shard_map/ppermute | solution.py:15
  204.5 3.4 collective-permute-start.6
  208.1 24.4 %collective-permute-done.3 = bf16[1,64,5120]{2,1,0:T(8,128)(2,1)S(1)} collective-permute-done((bf16[1,64,5120]{2,1,0:T(8,128)(2,1)S(1)}, bf16[1,64,5120]{2,1,0:T(8,128)(2,1)S(1)}, u32[]{:S(2)}, u32[]{:S(2)}) %collective-permute-start.3) | collective-permute-done | bytes 655392 | tf_op jit(solution)/shard_map/ppermute | solution.py:15
  235.1 16.6 %collective-permute-done.7 = bf16[2,32,5120]{2,1,0:T(8,128)(2,1)S(1)} collective-permute-done((bf16[2,32,5120]{2,1,0:T(8,128)(2,1)S(1)}, bf16[2,32,5120]{2,1,0:T(8,128)(2,1)S(1)}, u32[]{:S(2)}, u32[]{:S(2)}) %collective-permute-start.7) | collective-permute-done | bytes 655392 | tf_op jit(solution)/shard_map/ppermute | solution.py:15
  256.5 54.3 %collective-permute-done.8 = bf16[2,64,5120]{2,1,0:T(8,128)(2,1)S(1)} collective-permute-done((bf16[2,64,5120]{2,1,0:T(8,128)(2,1)S(1)}, bf16[2,64,5120]{2,1,0:T(8,128)(2,1)S(1)}, u32[]{:S(2)}, u32[]{:S(2)}) %collective-permute-start.8) | collective-permute-done | bytes 1310752 | tf_op jit(solution)/shard_map/ppermute | solution.py:15
  315.7 3.0 convolution_convert_fusion
  320.6 2.5 fusion.18
  331.2 3.4 fusion.20
  334.6 2.5 fusion.22
  337.1 4.5 %fusion = bf16[1,1,3,5120,128]{3,4,2,1,0:T(8,128)(2,1)} fusion(f32[3,128,5120]{2,1,0:T(8,128)S(1)} %fusion.22, bf16[4,128,128]{1,2,0:T(8,128)(2,1)} %collective-permute-done.10, bf16[3,128,5120]{2,1,0:T(8,128)(2,1)S(1)} %add_convert_fusion.2, bf16[2,128,5120]{2,1,0:T(8,128)(2,1)} %collective-permute-done.4), kind=kOutput, calls=%fused_computation.6 | convolution fusion | flops 515112960 | bytes 17170432 | tf_op jit(solution)/shard_map/sd,csn->cdn/dot_general | solution.py:156
  341.6 6.3 %copy.18 = bf16[1,1,3,5120,128]{4,3,2,1,0:T(8,128)(2,1)} copy(bf16[1,1,3,5120,128]{3,4,2,1,0:T(8,128)(2,1)} %fusion) | data formatting | bytes 7864320
  347.9 11.0 %collective-permute-done.12 = bf16[128,5120]{1,0:T(8,128)(2,1)} collective-permute-done((bf16[128,5120]{1,0:T(8,128)(2,1)}, bf16[128,5120]{1,0:T(8,128)(2,1)}, u32[]{:S(2)}, u32[]{:S(2)}) %collective-permute-start.12) | collective-permute-done | bytes 1310752 | tf_op jit(solution)/shard_map/ppermute | solution.py:30
  358.9 3.7 fusion.7
  362.6 7.5 %reduce-scatter.5.cloned.1.call-done = bf16[2,32,5120]{2,1,0:T(8,128)(2,1)} async-done(((bf16[2,128,5120]{2,1,0:T(8,128)(2,1)}), bf16[2,32,5120]{2,1,0:T(8,128)(2,1)}) %reduce-scatter.5.cloned.1.call-update) | async-done | bytes 655376 | tf_op jit(solution)/shard_map/reduce_scatter | solution.py:260
  (188 shorter events, 49.2 us)
Async XLA Ops:
  7.2 184.5 %reduce-scatter.3.cloned.1.call-start = ((), (), s32[]{:S(2)}) async-start(), calls=%async_computation.2 | async-start | bytes 3276800 | tf_op jit(solution)/shard_map/reduce_scatter | solution.py:260
  13.4 25.0 %collective-permute-start = (bf16[3,32,5120]{2,1,0:T(8,128)(2,1)S(1)}, bf16[3,32,5120]{2,1,0:T(8,128)(2,1)}, u32[]{:S(2)}, u32[]{:S(2)}) collective-permute-start(bf16[3,32,5120]{2,1,0:T(8,128)(2,1)S(1)} %pad_maximum_fusion.3), channel_id=1, source_target_pairs={{0,2},{2,0},{4,6},{6,4},{1,3},{3,1},{5,7},{7,5},{8,10},{10,8},{12,... | collective-permute-start | bytes 2949128 | tf_op jit(solution)/shard_map/ppermute | solution.py:15
  40.8 87.2 %collective-permute-start.1 = (bf16[3,64,5120]{2,1,0:T(8,128)(2,1)S(1)}, bf16[3,64,5120]{2,1,0:T(8,128)(2,1)}, u32[]{:S(2)}, u32[]{:S(2)}) collective-permute-start(bf16[3,64,5120]{2,1,0:T(8,128)(2,1)S(1)} %maximum_select_fusion.2), channel_id=1, source_target_pairs={{0,4},{2,6},{4,0},{6,2},{1,5},{3,7},{5,1},{7,3},{8,12},{10,14},{12... | collective-permute-start | bytes 5898248 | tf_op jit(solution)/shard_map/ppermute | solution.py:15
  51.8 83.5 %copy-start.4 = (bf16[1,384,5120]{2,1,0:T(8,128)(2,1)}, bf16[1,384,5120]{2,1,0:T(8,128)(2,1)S(1)}, u32[]{:S(2)}) copy-start(bf16[1,384,5120]{2,1,0:T(8,128)(2,1)S(1)} %pad_bitcast_fusion) | copy-start | bytes 11796484
  51.8 79.0 %copy-start.12 = (bf16[1,1,3,5120,128]{4,3,2,1,0:T(8,128)(2,1)S(1)}, bf16[1,1,3,5120,128]{4,3,2,1,0:T(8,128)(2,1)}, u32[]{:S(2)}) copy-start(bf16[1,1,3,5120,128]{4,3,2,1,0:T(8,128)(2,1)} %param.16) | copy-start | bytes 11796484
  138.3 231.8 %reduce-scatter.5.cloned.1.call-start = ((), (), s32[]{:S(2)}) async-start(), calls=%async_computation.3 | async-start | bytes 3276800 | tf_op jit(solution)/shard_map/reduce_scatter | solution.py:260
  139.7 53.1 %copy-start.17 = (bf16[32,5120]{1,0:T(8,128)(2,1)S(1)}, bf16[32,5120]{1,0:T(8,128)(2,1)}, u32[]{:S(2)}) copy-start(bf16[32,5120]{1,0:T(8,128)(2,1)} %get-tuple-element.14) | copy-start | bytes 983044
  139.7 53.9 %copy-start.22 = (bf16[1,2,32,5120]{3,2,1,0:T(8,128)(2,1)S(1)}, bf16[1,2,32,5120]{3,2,1,0:T(8,128)(2,1)}, u32[]{:S(2)}) copy-start(bf16[1,2,32,5120]{3,2,1,0:T(8,128)(2,1)} %param.21) | copy-start | bytes 1966084
  139.7 53.9 %copy-start.28 = (bf16[1,1,32,5120]{3,2,1,0:T(8,128)(2,1)S(1)}, bf16[1,1,32,5120]{3,2,1,0:T(8,128)(2,1)}, u32[]{:S(2)}) copy-start(bf16[1,1,32,5120]{3,2,1,0:T(8,128)(2,1)} %param.19) | copy-start | bytes 983044
  143.3 61.1 %copy-start.11 = (f32[32,5120]{1,0:T(8,128)S(1)}, f32[32,5120]{1,0:T(8,128)}, u32[]{:S(2)}) copy-start(f32[32,5120]{1,0:T(8,128)} %copy-done.10) | copy-start | bytes 1966084
  143.3 90.4 %collective-permute-start.4 = (bf16[2,128,5120]{2,1,0:T(8,128)(2,1)}, bf16[2,128,5120]{2,1,0:T(8,128)(2,1)}, u32[]{:S(2)}, u32[]{:S(2)}) collective-permute-start(bf16[2,128,5120]{2,1,0:T(8,128)(2,1)} %stack.115), channel_id=1, source_target_pairs={{0,25},{1,24},{8,17},{9,16},{16,9},{17,8},{24,1},{25,0},{2,27},{3,... | collective-permute-start | bytes 7864328 | tf_op jit(solution)/shard_map/ppermute | solution.py:30
  145.2 59.3 %copy-start.43 = (bf16[128,128]{1,0:T(8,128)(2,1)}, bf16[128,128]{1,0:T(8,128)(2,1)S(1)}, u32[]{:S(2)}) copy-start(bf16[128,128]{1,0:T(8,128)(2,1)S(1)} %convolution_convert_fusion.8) | copy-start | bytes 98308
  192.8 9.1 %collective-permute-start.2 = (bf16[1,32,5120]{2,1,0:T(8,128)(2,1)S(1)}, bf16[1,32,5120]{2,1,0:T(8,128)(2,1)S(1)}, u32[]{:S(2)}, u32[]{:S(2)}) collective-permute-start(bf16[1,32,5120]{2,1,0:T(8,128)(2,1)S(1)} %bitcast.361), channel_id=1, source_target_pairs={{0,2},{2,0},{4,6},{6,4},{1,3},{3,1},{5,7},{7,5},{8,10},{10,8},{12,... | collective-permute-start | bytes 983048 | tf_op jit(solution)/shard_map/ppermute | solution.py:15
  194.0 39.8 %collective-permute-start.5 = (bf16[32,5120]{1,0:T(8,128)(2,1)S(1)}, bf16[32,5120]{1,0:T(8,128)(2,1)S(1)}, u32[]{:S(2)}, u32[]{:S(2)}) collective-permute-start(bf16[32,5120]{1,0:T(8,128)(2,1)S(1)} %fusion.75), channel_id=1, source_target_pairs={{1,9},{8,0},{9,17},{16,8},{17,25},{24,16},{3,11},{10,2},{11,19},{1... | collective-permute-start | bytes 983048 | tf_op jit(solution)/shard_map/ppermute | solution.py:274
  202.1 30.4 %collective-permute-start.3 = (bf16[1,64,5120]{2,1,0:T(8,128)(2,1)S(1)}, bf16[1,64,5120]{2,1,0:T(8,128)(2,1)S(1)}, u32[]{:S(2)}, u32[]{:S(2)}) collective-permute-start(bf16[1,64,5120]{2,1,0:T(8,128)(2,1)S(1)} %maximum_select_fusion.7), channel_id=1, source_target_pairs={{0,4},{2,6},{4,0},{6,2},{1,5},{3,7},{5,1},{7,3},{8,12},{10,14},{12... | collective-permute-start | bytes 1966088 | tf_op jit(solution)/shard_map/ppermute | solution.py:15
  204.5 29.2 %collective-permute-start.6 = (bf16[32,5120]{1,0:T(8,128)(2,1)S(1)}, bf16[32,5120]{1,0:T(8,128)(2,1)S(1)}, u32[]{:S(2)}, u32[]{:S(2)}) collective-permute-start(bf16[32,5120]{1,0:T(8,128)(2,1)S(1)} %fusion.87), channel_id=1, source_target_pairs={{0,8},{8,16},{9,1},{16,24},{17,9},{25,17},{2,10},{10,18},{11,3},{1... | collective-permute-start | bytes 983048 | tf_op jit(solution)/shard_map/ppermute | solution.py:275
  235.0 16.7 %collective-permute-start.7 = (bf16[2,32,5120]{2,1,0:T(8,128)(2,1)S(1)}, bf16[2,32,5120]{2,1,0:T(8,128)(2,1)S(1)}, u32[]{:S(2)}, u32[]{:S(2)}) collective-permute-start(bf16[2,32,5120]{2,1,0:T(8,128)(2,1)S(1)} %pad_maximum_fusion.4), channel_id=1, source_target_pairs={{0,2},{2,0},{4,6},{6,4},{1,3},{3,1},{5,7},{7,5},{8,10},{10,8},{12,... | collective-permute-start | bytes 1966088 | tf_op jit(solution)/shard_map/ppermute | solution.py:15
  251.9 58.9 %collective-permute-start.8 = (bf16[2,64,5120]{2,1,0:T(8,128)(2,1)S(1)}, bf16[2,64,5120]{2,1,0:T(8,128)(2,1)S(1)}, u32[]{:S(2)}, u32[]{:S(2)}) collective-permute-start(bf16[2,64,5120]{2,1,0:T(8,128)(2,1)S(1)} %maximum_select_fusion.4), channel_id=1, source_target_pairs={{0,4},{2,6},{4,0},{6,2},{1,5},{3,7},{5,1},{7,3},{8,12},{10,14},{12... | collective-permute-start | bytes 3932168 | tf_op jit(solution)/shard_map/ppermute | solution.py:15
  252.7 66.0 %collective-permute-start.9 = (bf16[1,128,5120]{2,1,0:T(8,128)(2,1)}, bf16[1,128,5120]{2,1,0:T(8,128)(2,1)}, u32[]{:S(2)}, u32[]{:S(2)}) collective-permute-start(bf16[1,128,5120]{2,1,0:T(8,128)(2,1)} %maximum_select_fusion.3), channel_id=1, source_target_pairs={{0,25},{1,24},{8,17},{9,16},{16,9},{17,8},{24,1},{25,0},{2,27},{3,... | collective-permute-start | bytes 3932168 | tf_op jit(solution)/shard_map/ppermute | solution.py:30
  253.3 65.5 %collective-permute-start.10 = (bf16[4,128,128]{1,2,0:T(8,128)(2,1)}, bf16[4,128,128]{1,2,0:T(8,128)(2,1)}, u32[]{:S(2)}, u32[]{:S(2)}) collective-permute-start(bf16[4,128,128]{1,2,0:T(8,128)(2,1)} %pad_maximum_fusion.5), channel_id=1, source_target_pairs={{0,25},{1,24},{8,17},{9,16},{16,9},{17,8},{24,1},{25,0},{2,27},{3,... | collective-permute-start | bytes 393224 | tf_op jit(solution)/shard_map/ppermute | solution.py:30
  256.2 57.6 %copy-start.44 = (bf16[3,128,128]{2,1,0:T(8,128)(2,1)}, bf16[3,128,128]{2,1,0:T(8,128)(2,1)S(1)}, u32[]{:S(2)}) copy-start(bf16[3,128,128]{2,1,0:T(8,128)(2,1)S(1)} %fusion.41) | copy-start | bytes 294916
  256.5 55.0 %copy-start.24 = (bf16[1,1,128,5120]{3,2,1,0:T(8,128)(2,1)S(1)}, bf16[1,1,128,5120]{3,2,1,0:T(8,128)(2,1)}, u32[]{:S(2)}) copy-start(bf16[1,1,128,5120]{3,2,1,0:T(8,128)(2,1)} %param.17) | copy-start | bytes 3932164
  324.1 10.5 %collective-permute-start.11 = (bf16[4,128,128]{1,2,0:T(8,128)(2,1)S(1)}, bf16[4,128,128]{1,2,0:T(8,128)(2,1)S(1)}, u32[]{:S(2)}, u32[]{:S(2)}) collective-permute-start(bf16[4,128,128]{1,2,0:T(8,128)(2,1)S(1)} %pad_maximum_fusion.6), channel_id=1, source_target_pairs={{0,25},{1,24},{8,17},{9,16},{16,9},{17,8},{24,1},{25,0},{2,27},{3,... | collective-permute-start | bytes 393224 | tf_op jit(solution)/shard_map/ppermute | solution.py:30
  327.2 31.7 %collective-permute-start.12 = (bf16[128,5120]{1,0:T(8,128)(2,1)}, bf16[128,5120]{1,0:T(8,128)(2,1)}, u32[]{:S(2)}, u32[]{:S(2)}) collective-permute-start(bf16[128,5120]{1,0:T(8,128)(2,1)} %slice_bitcast_fusion.6), channel_id=1, source_target_pairs={{0,25},{1,24},{8,17},{9,16},{16,9},{17,8},{24,1},{25,0},{2,27},{3,... | collective-permute-start | bytes 3932168 | tf_op jit(solution)/shard_map/ppermute | solution.py:30
  (38 other events, 257.0 us)
Sparse Core Ops, SparseCore 0:
  138.5 53.2 reduce-scatter.2
  318.9 51.1 reduce-scatter.4
